TPU v7x, 32 devices: a whole 2x2x4 slice. The times are simulated.
32 devices in a mesh: grp: 2 (over y), seq: 4 (over z), head: 2 (over x), sub: 2 (over core).
Axes of the slice: x: 2, y: 2, z: 4, core: 2. Of those that a mesh axis runs over, the one named last changes fastest.
Arguments:
- query_rows: bfloat16 [3072, 1024], P(('grp', 'seq', 'sub'), 'head'), parts along dimension 0, may hold values from -8 to 8
- key_rows: bfloat16 [3072, 1024], P(('grp', 'seq', 'sub'), 'head'), parts along dimension 0, may hold values from -8 to 8
- value_rows: bfloat16 [3072, 1024], P(('grp', 'seq', 'sub'), 'head'), parts along dimension 0, may hold values from -8 to 8
- clip_lengths: int32 [12], P('grp'), parts along dimension 0, may hold values from 1 to 768, 1536 in all
- block_mask: int32 [48, 24], P(('grp', 'seq')), parts along dimension 0, may hold values from 0 to 1, as said below
- out_weight: bfloat16 [1024, 1024], replicated
- norm_gain: bfloat16 [1024], P('head'), may hold values from 0.099609375 to 1.8984375
Outputs:
- layer_output: bfloat16 [3072, 1024], P(('grp', 'seq', 'sub'), 'head'), parts along dimension 0
There are 2 independent parts, one for each index of `grp`. A program takes and returns all parts, laid end to end along the dimension named above; an argument that names none is the same for every part. Nothing has to cross between parts.
Inputs may be any that keep to these rules, and one draw needn't show every extreme that they name: `clip_lengths`: 6 clip lengths that sum to 1536; the longest is exactly 768. block_mask[i, i] = 1 for every block i.
All inputs are finite; a program needn't handle non-finite values.
Results may differ from a plain program's by a relative error of at most 0.01.
Values may be sent and summed in bfloat16 or wider, within the bound.
No kernel may reach another device: no remote copies, remote signals or barrier semaphores. Data moves between devices by JAX's collectives and lax.ppermute only.
A program may use at most 64 MiB of HBM per device.

v0:
```python
import math

import jax
import jax.numpy as jnp
from jax import lax
from jax.sharding import PartitionSpec as P

D = 1024
HD = 64
BLK = 64
F = 64


def padded_2(cells, sides, width):
    for axis, dim in sides:
        count = lax.axis_size(axis)
        ends = count - 1
        head = lax.slice_in_dim(cells, 0, width, axis=dim)
        tail = lax.slice_in_dim(cells, cells.shape[dim] - width, cells.shape[dim], axis=dim)
        cells = jnp.concatenate(
            [
                lax.ppermute(tail, axis, [(i, (i + 1) % count) for i in range(ends)]),
                cells,
                lax.ppermute(head, axis, [((i + 1) % count, i) for i in range(ends)]),
            ],
            axis=dim,
        )
    return cells


def clip_index(positions, clip_ends):
    return jnp.sum((clip_ends[None, :] <= positions[:, None]).astype(jnp.int32), axis=1)


def make_attention(queries, first_row, mask_rows, clip_ends):
    row_count, col_count = queries.shape
    head_count = col_count // HD
    per_head = queries.reshape(row_count, head_count, HD)
    query_clip = clip_index(first_row + jnp.arange(row_count, dtype=jnp.int32), clip_ends)
    mask_float = mask_rows.astype(jnp.float32)
    block_total = mask_rows.shape[1]
    score_scale = 1.0 / math.sqrt(HD)

    def key_block(state_now, key_part, value_part, part_start):
        part_rows = key_part.shape[0]
        key_pos = part_start + jnp.arange(part_rows, dtype=jnp.int32)
        one_hot = (
            (key_pos // BLK)[:, None] == jnp.arange(block_total, dtype=jnp.int32)[None, :]
        ).astype(jnp.float32)
        block_live = jnp.dot(mask_float, one_hot.T, precision=lax.Precision.HIGHEST) > 0.5
        allowed = jnp.repeat(block_live, BLK, axis=0) & (
            query_clip[:, None] == clip_index(key_pos, clip_ends)[None, :]
        )
        row_max, running, weighted = state_now
        scores = (
            jnp.einsum(
                "rhd,khd->hrk",
                per_head,
                key_part.reshape(part_rows, head_count, HD),
                preferred_element_type=jnp.float32,
            )
            * score_scale
        )
        scores = jnp.where(allowed[None], scores, -1e30)
        new_max = jnp.maximum(row_max, jnp.max(scores, axis=2))
        weights_now = jnp.where(allowed[None], jnp.exp(scores - new_max[:, :, None]), 0.0)
        rescale = jnp.exp(row_max - new_max)
        running = running * rescale + jnp.sum(weights_now, axis=2)
        update = jnp.einsum(
            "hrk,khd->rhd",
            weights_now.astype(jnp.bfloat16),
            value_part.reshape(part_rows, head_count, HD),
            preferred_element_type=jnp.float32,
        )
        weighted = weighted * jnp.repeat(rescale.T, HD, axis=1) + update.reshape(
            row_count, col_count
        )
        return (new_max, running, weighted)

    def fold_step(state_now, piece, piece_start):
        key_piece, value_piece = piece
        piece_rows = key_piece.shape[0]
        full_count = piece_rows // 1024

        def loop_step(step_index, state_in):
            offset = step_index * 1024
            return key_block(
                state_in,
                lax.dynamic_slice_in_dim(key_piece, offset, 1024, 0),
                lax.dynamic_slice_in_dim(value_piece, offset, 1024, 0),
                offset,
            )

        state_now = lax.fori_loop(0, full_count, loop_step, state_now)
        remain = piece_rows - full_count * 1024
        if remain > 0:
            tail_start = full_count * 1024
            state_now = key_block(
                state_now,
                key_piece[tail_start:],
                value_piece[tail_start:],
                piece_start + tail_start,
            )
        return state_now

    initial = (
        jnp.full((head_count, row_count), -1e30, jnp.float32),
        jnp.zeros((head_count, row_count), jnp.float32),
        jnp.zeros((row_count, col_count), jnp.float32),
    )

    def finish(state_now):
        row_max, running, weighted = state_now
        return (weighted / jnp.repeat(running.T, HD, axis=1)).astype(jnp.bfloat16)

    return (fold_step, initial, finish)


def body(query_rows, key_rows, value_rows, clip_lengths, block_mask, out_weight, norm_gain):
    row_count, col_count = query_rows.shape
    clip_ends = jnp.cumsum(clip_lengths)
    token_first = (lax.axis_index("seq") * lax.axis_size("sub") + lax.axis_index("sub")) * row_count
    mask_height = row_count // BLK
    mask_rows = lax.dynamic_slice_in_dim(
        block_mask, lax.axis_index("sub") * mask_height, mask_height, 0
    )
    fold_step, initial, finish = make_attention(query_rows, token_first, mask_rows, clip_ends)
    folded = fold_step(
        initial,
        (
            lax.all_gather(key_rows, ("seq", "sub"), axis=0, tiled=True),
            lax.all_gather(value_rows, ("seq", "sub"), axis=0, tiled=True),
        ),
        jnp.int32(0),
    )
    attended = finish(folded)
    head_index = lax.axis_index("head")
    weight_rows = lax.dynamic_slice_in_dim(out_weight, head_index * col_count, col_count, 0)
    projected = lax.psum_scatter(
        jnp.dot(attended, weight_rows, preferred_element_type=jnp.float32).astype(jnp.bfloat16),
        "head",
        scatter_dimension=1,
        tiled=True,
    ).astype(jnp.float32)
    padded = padded_2(projected.astype(jnp.bfloat16), ((("seq", "sub"), 0),), F).astype(
        projected.dtype
    )
    positions = token_first + jnp.arange(row_count, dtype=jnp.int32)
    clip_here = clip_index(positions, clip_ends)
    earlier = jnp.where(
        (clip_index(positions - F, clip_ends) == clip_here)[:, None], padded[:row_count], 0.0
    )
    later = jnp.where(
        (clip_index(positions + F, clip_ends) == clip_here)[:, None], padded[2 * F :], 0.0
    )
    blended = projected + 0.5 * (earlier + later)
    squares = lax.psum(jnp.sum(blended * blended, axis=1), "head")
    scaled = blended * lax.rsqrt(squares / D + 1e-06)[:, None]
    return (scaled * norm_gain.astype(jnp.float32)).astype(jnp.bfloat16)


def solution(mesh):
    placed = (
        P(("grp", "seq", "sub"), "head"),
        P(("grp", "seq", "sub"), "head"),
        P(("grp", "seq", "sub"), "head"),
        P("grp"),
        P(("grp", "seq"), None),
        P(),
        P("head"),
    )
    return jax.shard_map(
        body,
        mesh=mesh,
        in_specs=placed,
        out_specs=P(("grp", "seq", "sub"), "head"),
        check_vma=False,
    )
```

profile of v0, /device:TPU:20, one launch (start us, length us, event | category | flops | bytes accessed | tf_op | source)
XLA Modules:
  0.0 115.2 jit_solution(12509582171449820308)
XLA Ops:
  6.5 0.0 copy-start
  6.5 0.0 all-gather.5.cloned.1.call-start
  6.5 0.7 all-gather.5.cloned.1.call-update
  7.3 0.0 all-gather.3.cloned.1.call-start
  7.3 0.7 all-gather.3.cloned.1.call-update
  8.0 0.0 reduce-scatter.2.cloned.1.call-start
  8.1 0.8 reduce-window.8
  8.9 1.1 copy.19
  10.0 0.1 convert_reduce_fusion.1
  10.1 0.1 convert_reduce_fusion.3
  10.2 1.0 convolution_compare_fusion.1
  11.2 0.1 compare_and_fusion.1
  11.4 0.1 convert_reduce_fusion
  11.4 1.1 convolution_compare_fusion
  12.6 0.9 compare_and_fusion
  13.5 20.9 %all-gather.5.cloned.1.call-done = bf16[1536,512]{1,0:T(8,128)(2,1)} async-done(((bf16[192,512]{1,0:T(8,128)(2,1)}), bf16[1536,512]{1,0:T(8,128)(2,1)}) %all-gather.5.cloned.1.call-update) | async-done | bytes 1572880 | tf_op jit(solution)/shard_map/all_gather | solution.py:132
  34.4 1.3 %dynamic_slice.19 = bf16[1024,512]{1,0:T(8,128)(2,1)S(1)} slice(bf16[1536,512]{1,0:T(8,128)(2,1)} %all-gather.5.cloned.1.call-done), slice={[0:1024], [0:512]} | slice | bytes 2097152 | tf_op jit(solution)/shard_map/while/body/eval_jaxpr/dynamic_slice | solution.py:90
  35.7 1.3 %copy.21 = bf16[1024,512]{0,1:T(8,128)(2,1)} copy(bf16[1024,512]{1,0:T(8,128)(2,1)S(1)} %dynamic_slice.19) | data formatting | bytes 2097152 | tf_op jit(solution)/shard_map/while/body/eval_jaxpr/dynamic_slice | solution.py:90
  37.0 1.1 slice.27
  38.1 1.0 copy.23
  39.1 21.5 %all-gather.3.cloned.1.call-done = bf16[1536,512]{1,0:T(8,128)(2,1)} async-done(((bf16[192,512]{1,0:T(8,128)(2,1)}), bf16[1536,512]{1,0:T(8,128)(2,1)}) %all-gather.3.cloned.1.call-update) | async-done | bytes 1572880 | tf_op jit(solution)/shard_map/all_gather | solution.py:131
  60.6 2.3 %dynamic_slice.18 = bf16[1024,512]{1,0:T(8,128)(2,1)} slice(bf16[1536,512]{1,0:T(8,128)(2,1)} %all-gather.3.cloned.1.call-done), slice={[0:1024], [0:512]} | slice | bytes 2097152 | tf_op jit(solution)/shard_map/while/body/eval_jaxpr/dynamic_slice | solution.py:89
  62.9 1.5 %copy.20 = bf16[1024,512]{0,1:T(8,128)(2,1)S(1)} copy(bf16[1024,512]{1,0:T(8,128)(2,1)} %dynamic_slice.18) | data formatting | bytes 2097152 | tf_op jit(solution)/shard_map/while/body/eval_jaxpr/dynamic_slice | solution.py:89
  64.4 1.9 %slice.26 = bf16[512,512]{1,0:T(8,128)(2,1)} slice(bf16[1536,512]{1,0:T(8,128)(2,1)} %all-gather.3.cloned.1.call-done), slice={[1024:1536], [0:512]} | slice | bytes 1048576 | tf_op jit(solution)/shard_map/slice | solution.py:100
  66.3 2.1 %copy.22 = bf16[512,512]{0,1:T(8,128)(2,1)} copy(bf16[512,512]{1,0:T(8,128)(2,1)} %slice.26) | data formatting | bytes 1048576 | tf_op jit(solution)/shard_map/slice | solution.py:100
  68.3 0.0 copy-start.1
  68.3 1.9 %fusion.6 = (f32[8,192]{1,0:T(8,128)S(1)}, f32[8,192,512]{2,1,0:T(8,128)S(1)}) fusion(pred[192,512]{1,0:T(8,128)(4,1)S(1)} %compare_and_fusion.1, bf16[192,8,64]{0,2,1:T(8,128)(2,1)S(1)} %bitcast.55, bf16[512,8,64]{0,2,1:T(8,128)(2,1)} %bitcast.57), kind=kOutput, calls=%fused_computation.9 | convolution fusion | flops 103021056 | bytes 3971072 | tf_op jit(solution)/shard_map/rhd,khd->hrk/dot_general | solution.py:56
  70.2 0.0 copy-done.1
  70.2 1.3 %fusion = (f32[8,192]{1,0:T(8,128)S(1)}, f32[8,192,1024]{2,1,0:T(8,128)S(1)}) fusion(pred[192,1024]{1,0:T(8,128)(4,1)S(1)} %copy-done.1, bf16[192,8,64]{0,2,1:T(8,128)(2,1)S(1)} %bitcast.56, bf16[1024,8,64]{0,2,1:T(8,128)(2,1)S(1)} %bitcast.54), kind=kOutput, calls=%fused_computation.2 | convolution fusion | flops 206043648 | bytes 7739392 | tf_op jit(solution)/shard_map/while/body/eval_jaxpr/rhd,khd->hrk/dot_general | solution.py:56
  71.5 1.1 fusion.7
  72.6 0.0 copy-start.2
  72.6 2.1 %fusion.1 = f32[8,192]{1,0:T(8,128)S(1)} fusion(f32[8,192,1024]{2,1,0:T(8,128)S(1)} %get-tuple-element.55, f32[8,192]{1,0:T(8,128)S(1)} %get-tuple-element.49, pred[192,1024]{1,0:T(8,128)(4,1)S(1)} %copy-done.1), kind=kLoop, calls=%fused_computation.3 | loop fusion | flops 7862784 | bytes 6500352 | tf_op jit(solution)/shard_map/while/body/eval_jaxpr/reduce_sum | solution.py:68
  74.7 0.0 copy-done.2
  74.8 0.0 copy-start.3
  74.8 1.8 %fusion.21 = f32[192,8,64]{0,2,1:T(8,128)S(1)} fusion(bf16[1024,8,64]{0,2,1:T(8,128)(2,1)S(1)} %bitcast.58, f32[8,192,1024]{2,1,0:T(8,128)S(1)} %get-tuple-element.55, f32[8,192]{1,0:T(8,128)S(1)} %get-tuple-element.49, pred[192,1024]{1,0:T(8,128)(4,1)S(1)} %copy-done.1, f32[192,8]{0,1:T(8,128)S(1)} %get-tuple-element.31, f32[192,8]{0,1:T(8,128)S(1)} %get-tuple-element.46), kind=kOutput, calls=%fused_computation.18 | convolution fusion | flops 209387520 | bytes 7948288 | tf_op jit(solution)/shard_map/while/body/eval_jaxpr/hrk,khd->rhd/dot_general | solution.py:69
  76.6 0.0 copy-done.3
  76.6 0.0 copy-start.4
  76.6 1.0 fusion.31
  77.7 0.0 copy-done
  77.7 1.1 convolution_convert_fusion
  78.8 0.0 reduce-scatter.2.cloned.1.call-update
  78.8 13.5 %reduce-scatter.2.cloned.1.call-done = bf16[192,512]{1,0:T(8,128)(2,1)} async-done(((bf16[192,1024]{1,0:T(8,128)(2,1)}), bf16[192,512]{1,0:T(8,128)(2,1)}) %reduce-scatter.2.cloned.1.call-update) | async-done | bytes 196624 | tf_op jit(solution)/shard_map/reduce_scatter | solution.py:139
  92.4 0.9 fusion.67
  93.2 1.9 %collective-permute-start = (bf16[64,512]{1,0:T(8,128)(2,1)S(1)}, bf16[64,512]{1,0:T(8,128)(2,1)S(1)}, u32[]{:S(2)}, u32[]{:S(2)}) collective-permute-start(bf16[64,512]{1,0:T(8,128)(2,1)S(1)} %get-tuple-element.32), channel_id=1, source_target_pairs={{0,1},{1,4},{4,5},{5,8},{8,9},{9,12},{12,13},{2,3},{3,6},{6,7},{7,... | collective-permute-start | bytes 196616 | tf_op jit(solution)/shard_map/ppermute | solution.py:22
  95.2 3.6 %collective-permute-start.1 = (bf16[64,512]{1,0:T(8,128)(2,1)S(1)}, bf16[64,512]{1,0:T(8,128)(2,1)S(1)}, u32[]{:S(2)}, u32[]{:S(2)}) collective-permute-start(bf16[64,512]{1,0:T(8,128)(2,1)S(1)} %get-tuple-element.44), channel_id=1, source_target_pairs={{1,0},{4,1},{5,4},{8,5},{9,8},{12,9},{13,12},{3,2},{6,3},{7,6},{10... | collective-permute-start | bytes 196616 | tf_op jit(solution)/shard_map/ppermute | solution.py:24
  98.8 0.0 copy-done.4
  98.9 0.0 collective-permute-done
  98.9 1.8 %collective-permute-done.1 = bf16[64,512]{1,0:T(8,128)(2,1)S(1)} collective-permute-done((bf16[64,512]{1,0:T(8,128)(2,1)S(1)}, bf16[64,512]{1,0:T(8,128)(2,1)S(1)}, u32[]{:S(2)}, u32[]{:S(2)}) %collective-permute-start.1) | collective-permute-done | bytes 65568 | tf_op jit(solution)/shard_map/ppermute | solution.py:24
  100.7 1.0 maximum_convert_fusion
  101.7 1.2 %multiply_reduce_fusion = (f32[192]{0:T(256)S(1)}, f32[192,512]{1,0:T(8,128)S(1)}) fusion(f32[320,512]{1,0:T(8,128)S(1)} %maximum_convert_fusion, pred[192]{0:T(512)(128)(4,1)S(1)} %get-tuple-element.51, pred[192]{0:T(512)(128)(4,1)S(1)} %get-tuple-element.50, bf16[192,512]{1,0:T(8,128)(2,1)} %reduce-scatter.2.cloned.1.call-done), kind=kLoop, calls=%fused_computation.33 | loop fusion | flops 786240 | bytes 1377408 | tf_op jit(solution)/shard_map/reduce_sum | solution.py:157
  102.9 4.9 %psum.7 = f32[192]{0:T(256)S(1)} all-reduce(f32[192]{0:T(256)S(1)} %get-tuple-element.28), channel_id=1, replica_groups=mesh['grp'=2,'seq'=4,'head'=2,'sub'=2] {'head'}, use_global_device_ids=true, to_apply=%region_12.13 | all-reduce | flops 192 | bytes 1536 | tf_op jit(solution)/shard_map/psum | solution.py:157
  107.9 0.8 multiply_convert_fusion
  (10 shorter events, 0.1 us)
Async XLA Ops:
  6.5 71.1 %copy-start = (bf16[1024,1024]{1,0:T(8,128)(2,1)S(1)}, bf16[1024,1024]{1,0:T(8,128)(2,1)}, u32[]{:S(2)}) copy-start(bf16[1024,1024]{1,0:T(8,128)(2,1)} %param.12) | copy-start | bytes 6291460
  6.5 27.8 %all-gather.5.cloned.1.call-start = ((), (), s32[]{:S(2)}) async-start(), calls=%async_computation.2 | async-start | bytes 1769472 | tf_op jit(solution)/shard_map/all_gather | solution.py:132
  7.3 53.4 %all-gather.3.cloned.1.call-start = ((), (), s32[]{:S(2)}) async-start(), calls=%async_computation.1 | async-start | bytes 1769472 | tf_op jit(solution)/shard_map/all_gather | solution.py:131
  8.0 84.4 %reduce-scatter.2.cloned.1.call-start = ((), (), s32[]{:S(2)}) async-start(), calls=%async_computation.3 | async-start | bytes 589824 | tf_op jit(solution)/shard_map/reduce_scatter | solution.py:139
  68.3 1.9 %copy-start.1 = (pred[192,1024]{1,0:T(8,128)(4,1)S(1)}, pred[192,1024]{1,0:T(8,128)(4,1)}, u32[]{:S(2)}) copy-start(pred[192,1024]{1,0:T(8,128)(4,1)} %compare_and_fusion) | copy-start | bytes 589828
  72.6 2.1 %copy-start.2 = (bf16[1024,512]{0,1:T(8,128)(2,1)S(1)}, bf16[1024,512]{0,1:T(8,128)(2,1)}, u32[]{:S(2)}) copy-start(bf16[1024,512]{0,1:T(8,128)(2,1)} %copy.21) | copy-start | bytes 3145732
  74.8 1.8 %copy-start.3 = (bf16[512,512]{0,1:T(8,128)(2,1)S(1)}, bf16[512,512]{0,1:T(8,128)(2,1)}, u32[]{:S(2)}) copy-start(bf16[512,512]{0,1:T(8,128)(2,1)} %copy.23) | copy-start | bytes 1572868
  76.6 22.2 %copy-start.4 = (bf16[512]{0:T(512)(128)(2,1)S(1)}, bf16[512]{0:T(512)(128)(2,1)}, u32[]{:S(2)}) copy-start(bf16[512]{0:T(512)(128)(2,1)} %param.13) | copy-start | bytes 3076
  93.2 5.6 %collective-permute-start = (bf16[64,512]{1,0:T(8,128)(2,1)S(1)}, bf16[64,512]{1,0:T(8,128)(2,1)S(1)}, u32[]{:S(2)}, u32[]{:S(2)}) collective-permute-start(bf16[64,512]{1,0:T(8,128)(2,1)S(1)} %get-tuple-element.32), channel_id=1, source_target_pairs={{0,1},{1,4},{4,5},{5,8},{8,9},{9,12},{12,13},{2,3},{3,6},{6,7},{7,... | collective-permute-start | bytes 196616 | tf_op jit(solution)/shard_map/ppermute | solution.py:22
  95.2 5.5 %collective-permute-start.1 = (bf16[64,512]{1,0:T(8,128)(2,1)S(1)}, bf16[64,512]{1,0:T(8,128)(2,1)S(1)}, u32[]{:S(2)}, u32[]{:S(2)}) collective-permute-start(bf16[64,512]{1,0:T(8,128)(2,1)S(1)} %get-tuple-element.44), channel_id=1, source_target_pairs={{1,0},{4,1},{5,4},{8,5},{9,8},{12,9},{13,12},{3,2},{6,3},{7,6},{10... | collective-permute-start | bytes 196616 | tf_op jit(solution)/shard_map/ppermute | solution.py:24
Sparse Core Ops, SparseCore 0:
  9.0 25.3 all-gather.4
  36.0 24.5 all-gather.2
  79.0 13.3 reduce-scatter.1
where the time goes:
time: 118 us; the launch traced here: 115 us
  waiting for transfers between devices  59.2 us (50%)
  local copies, waits for them, and re-layouts  14.4 us (12%)
  between operations  13.3 us (11%)
  matrix products  9.32 us (8%)
  other arithmetic  8.35 us (7%)
  starting transfers between devices  5.64 us (5%)
  blocking collectives  4.94 us (4%)
    all_gather x1, waiting for transfers between devices, body(): lax.all_gather(key_rows, ('seq', 'sub'), axis=0, tiled=True)  21.5 us
    all_gather x1, waiting for transfers between devices, body(): lax.all_gather(value_rows, ('seq', 'sub'), axis=0, tiled=True)  20.9 us
    reduce_scatter x1, waiting for transfers between devices, body(): lax.psum_scatter(jnp.dot(attended, weight_rows, preferred_element_type=jn...  13.5 us
    psum x1, blocking collectives, body(): squares = lax.psum(jnp.sum(blended * blended, axis=1), 'head')  4.94 us
    slice x2, local copies, waits for them, and re-layouts, fold_step(): key_piece[tail_start:]  3.94 us
    dynamic_slice x2, local copies, waits for them, and re-layouts, loop_step(): lax.dynamic_slice_in_dim(key_piece, offset, 1024, 0)  3.74 us
    ppermute x1, starting transfers between devices, padded_2(): lax.ppermute(head, axis, [((i + 1) % count, i) for i in range(ends)])  3.64 us
    reduce_sum x2, other arithmetic, key_block(): running = running * rescale + jnp.sum(weights_now, axis=2)  3.18 us
  transfers between devices with their start and end apart: 5, of which 4 were waited for; matrix products, arithmetic and copies ran while one was open for 9% of the time, Pallas kernels for 0%

commit v1 on v0

v1 whole, which is shorter than its diff:
```python
import math

import jax
import jax.numpy as jnp
from jax import lax
from jax.sharding import PartitionSpec as P

HD = 64
BLK = 64
F = 64


def clip_index(positions, clip_ends):
    return jnp.sum((clip_ends[None, :] <= positions[:, None]).astype(jnp.int32), axis=1)


def shifted(x, axis, count, step):
    pairs = [(i + step, i) for i in range(count) if 0 <= i + step < count]
    return lax.ppermute(x, axis, pairs)


def rotated(x, axis, count, step):
    return lax.ppermute(x, axis, [(i, (i + step) % count) for i in range(count)])


def attend_chunk(state_now, per_head, query_clip, mask_float, clip_ends, keys, values, key_pos):
    row_count, head_count, _ = per_head.shape
    key_rows = keys.shape[0]
    block_total = mask_float.shape[1]
    one_hot = (
        (key_pos // BLK)[:, None] == jnp.arange(block_total, dtype=jnp.int32)[None, :]
    ).astype(jnp.float32)
    block_live = jnp.dot(mask_float, one_hot.T, precision=lax.Precision.HIGHEST) > 0.5
    allowed = jnp.repeat(block_live, BLK, axis=0) & (
        query_clip[:, None] == clip_index(key_pos, clip_ends)[None, :]
    )
    row_max, running, weighted = state_now
    scores = jnp.einsum(
        "rhd,khd->hrk",
        per_head,
        keys.reshape(key_rows, head_count, HD),
        preferred_element_type=jnp.float32,
    ) * (1.0 / math.sqrt(HD))
    scores = jnp.where(allowed[None], scores, -1e30)
    new_max = jnp.maximum(row_max, jnp.max(scores, axis=2))
    weights_now = jnp.where(allowed[None], jnp.exp(scores - new_max[:, :, None]), 0.0)
    rescale = jnp.exp(row_max - new_max)
    running = running * rescale + jnp.sum(weights_now, axis=2)
    update = jnp.einsum(
        "hrk,khd->rhd",
        weights_now.astype(jnp.bfloat16),
        values.reshape(key_rows, head_count, HD),
        preferred_element_type=jnp.float32,
    )
    weighted = weighted * jnp.repeat(rescale.T, HD, axis=1) + update.reshape(
        row_count, head_count * HD
    )
    return (new_max, running, weighted)


def body(query_rows, key_rows, value_rows, clip_lengths, block_mask, out_weight, norm_gain):
    row_count, col_count = query_rows.shape
    head_count = col_count // HD
    n_seq = lax.axis_size("seq")
    n_sub = lax.axis_size("sub")
    n_head = lax.axis_size("head")
    seq_i = lax.axis_index("seq")
    sub_i = lax.axis_index("sub")
    head_i = lax.axis_index("head")
    chip_rows = row_count * n_sub
    total = chip_rows * n_seq
    longest = total // 2
    reach = min(n_seq - 1, 1 + (longest - 2) // chip_rows)

    clip_ends = jnp.cumsum(clip_lengths)
    token_first = (seq_i * n_sub + sub_i) * row_count
    mask_height = row_count // BLK
    mask_rows = lax.dynamic_slice_in_dim(block_mask, sub_i * mask_height, mask_height, 0)
    mask_float = mask_rows.astype(jnp.float32)
    per_head = query_rows.reshape(row_count, head_count, HD)
    query_clip = clip_index(token_first + jnp.arange(row_count, dtype=jnp.int32), clip_ends)
    local_pos = jnp.arange(row_count, dtype=jnp.int32)

    def block_pos(seq_off, sub_src):
        return ((seq_i + seq_off) * n_sub + sub_src) * row_count + local_pos

    def partner_blocks(blocks):
        stacked = jnp.stack([kv for kv, _ in blocks])
        out = []
        for j in range(1, n_sub):
            got = rotated(stacked, "sub", n_sub, j)
            src = (sub_i - j) % n_sub
            out += [(got[b], off, src) for b, (_, off) in enumerate(blocks)]
        return out

    state = (
        jnp.full((head_count, row_count), -1e30, jnp.float32),
        jnp.zeros((head_count, row_count), jnp.float32),
        jnp.zeros((row_count, col_count), jnp.float32),
    )

    def fold(state_now, chunk):
        keys = jnp.concatenate([kv[0] for kv, _, _ in chunk], axis=0)
        values = jnp.concatenate([kv[1] for kv, _, _ in chunk], axis=0)
        key_pos = jnp.concatenate([block_pos(off, src) for _, off, src in chunk], axis=0)
        return attend_chunk(
            state_now, per_head, query_clip, mask_float, clip_ends, keys, values, key_pos
        )

    own = jnp.stack([key_rows, value_rows])
    mine = [(own, 0)]
    state = fold(state, [(own, 0, sub_i)] + partner_blocks(mine))

    def seq_step(step, carry):
        state_now, left, right = carry
        right = shifted(right, "seq", n_seq, 1)
        left = shifted(left, "seq", n_seq, -1)
        mine = [(left, -step), (right, step)]
        chunk = [(left, -step, sub_i), (right, step, sub_i)] + partner_blocks(mine)
        return (fold(state_now, chunk), left, right)

    carry = (state, own, own)
    if reach <= 4:
        for step in range(1, reach + 1):
            carry = seq_step(step, carry)
    else:
        carry = lax.fori_loop(1, reach + 1, seq_step, carry)
    state = carry[0]

    row_max, running, weighted = state
    attended = (weighted / jnp.repeat(running.T, HD, axis=1)).astype(jnp.bfloat16)

    n_dev = n_seq * n_sub
    prev_tail = shifted(attended[row_count - F :], ("seq", "sub"), n_dev, -1)
    next_head = shifted(attended[:F], ("seq", "sub"), n_dev, 1)
    extended = jnp.concatenate([prev_tail, attended, next_head], axis=0)

    projected = jnp.dot(
        extended,
        lax.dynamic_slice_in_dim(out_weight, head_i * col_count, col_count, 0),
        preferred_element_type=jnp.float32,
    )
    for j in range(1, n_head):
        got = rotated(extended, "head", n_head, j)
        src = (head_i - j) % n_head
        projected = projected + jnp.dot(
            got,
            lax.dynamic_slice_in_dim(out_weight, src * col_count, col_count, 0),
            preferred_element_type=jnp.float32,
        )

    positions = token_first + jnp.arange(row_count, dtype=jnp.int32)
    clip_here = clip_index(positions, clip_ends)
    earlier = jnp.where(
        (clip_index(positions - F, clip_ends) == clip_here)[:, None], projected[:row_count], 0.0
    )
    later = jnp.where(
        (clip_index(positions + F, clip_ends) == clip_here)[:, None], projected[2 * F :], 0.0
    )
    blended = projected[F : F + row_count] + 0.5 * (earlier + later)
    width = out_weight.shape[1]
    squares = jnp.sum(blended * blended, axis=1)
    scale = lax.rsqrt(squares / width + 1e-06)
    own_cols = lax.dynamic_slice_in_dim(blended, head_i * col_count, col_count, 1)
    return (own_cols * scale[:, None] * norm_gain.astype(jnp.float32)).astype(jnp.bfloat16)


def solution(mesh):
    placed = (
        P(("grp", "seq", "sub"), "head"),
        P(("grp", "seq", "sub"), "head"),
        P(("grp", "seq", "sub"), "head"),
        P("grp"),
        P(("grp", "seq"), None),
        P(),
        P("head"),
    )
    return jax.shard_map(
        body,
        mesh=mesh,
        in_specs=placed,
        out_specs=P(("grp", "seq", "sub"), "head"),
        check_vma=False,
    )
```

time: 118 us -> 102 us (0.86); the launches traced: 115 us -> 101 us
  waiting for transfers between devices: 59.2 us -> 13.2 us
  local copies, waits for them, and re-layouts: 14.4 us -> 32.7 us
  starting transfers between devices: 5.64 us -> 18.8 us
  between operations: 13.3 us -> 0.46 us
  matrix products: 9.32 us -> 20 us
  other arithmetic: 8.35 us -> 16.3 us
  blocking collectives: 4.94 us -> 0 us
    all_gather x2 -> x0, waiting for transfers between devices: 42.4 us -> none  [the longest x1 21.5 us: body(): lax.all_gather(key_rows, ('seq', 'sub'), axis=0, tiled=True)]
    slice x5 -> x26, local copies, waits for them, and re-layouts: 6.92 us -> 27.7 us  [the longest x16 17.4 us: fold(): values = jnp.concatenate([kv[1] for kv, _, _ in chunk], axis=0)]
    reduce_scatter x1 -> x0, waiting for transfers between devices: 13.5 us -> none  [body(): lax.psum_scatter(jnp.dot(attended, weight_rows, preferred_element_type=jn...]
    ppermute x2 -> x10, starting transfers between devices: 5.56 us -> 18.8 us  [the longest x6 16.8 us: shifted(): return lax.ppermute(x, axis, pairs)]
    ppermute x2 -> x10, waiting for transfers between devices: 1.84 us -> 13.2 us  [the longest x4 9.31 us: rotated(): lax.ppermute(x, axis, [(i, (i + step) % count) for i in range(count)])]
    dot_general x7 -> x11, matrix products: 9.32 us -> 20 us  [the longest x3 10.3 us: attend_chunk(): jnp.einsum('rhd,khd->hrk', per_head, keys.reshape(key_rows, head_count, H...]
    dynamic_slice x4 -> x0, local copies, waits for them, and re-layouts: 6.36 us -> none  [the longest x2 3.74 us: loop_step(): lax.dynamic_slice_in_dim(key_piece, offset, 1024, 0)]
    psum x1 -> x0, blocking collectives: 4.94 us -> none  [body(): squares = lax.psum(jnp.sum(blended * blended, axis=1), 'head')]
  transfers between devices with their start and end apart: 5 -> 10, of which waited for: 4 -> 3; matrix products, arithmetic and copies ran while one was open for 9% -> 48% of each run, Pallas kernels for 0% -> 0%
where the time goes in v1:
time: 102 us; the launch traced here: 101 us
  local copies, waits for them, and re-layouts  32.7 us (32%)
  matrix products  20 us (20%)
  starting transfers between devices  18.8 us (18%)
  other arithmetic  16.3 us (16%)
  waiting for transfers between devices  13.2 us (13%)
    slice x16, local copies, waits for them, and re-layouts, fold(): values = jnp.concatenate([kv[1] for kv, _, _ in chunk], axis=0)  17.4 us
    ppermute x6, starting transfers between devices, shifted(): return lax.ppermute(x, axis, pairs)  16.8 us
    dot_general x3, matrix products, attend_chunk(): jnp.einsum('rhd,khd->hrk', per_head, keys.reshape(key_rows, head_count, H...  10.3 us
    slice x9, local copies, waits for them, and re-layouts, fold(): keys = jnp.concatenate([kv[0] for kv, _, _ in chunk], axis=0)  10.3 us
    ppermute x4, waiting for transfers between devices, rotated(): lax.ppermute(x, axis, [(i, (i + step) % count) for i in range(count)])  9.31 us
    unnamed x45, local copies, waits for them, and re-layouts  4.94 us
    another operation x3, other arithmetic, partner_blocks(): stacked = jnp.stack([kv for kv, _ in blocks])  4.89 us
    dot_general x3, matrix products, attend_chunk(): jnp.dot(mask_float, one_hot.T, precision=lax.Precision.HIGHEST) > 0.5  4.31 us
  transfers between devices with their start and end apart: 10, of which 3 were waited for; matrix products, arithmetic and copies ran while one was open for 48% of the time, Pallas kernels for 0%

profile of v1, /device:TPU:20, one launch (start us, length us, event | category | flops | bytes accessed | tf_op | source)
XLA Modules:
  0.0 101.4 jit_solution(4144763045203920382)
XLA Ops:
  0.0 2.0 %fusion.120 = (bf16[1,2,192,512]{3,2,1,0:T(8,128)(2,1)}, bf16[2,192,512]{2,1,0:T(8,128)(2,1)S(1)}) fusion(bf16[1,192,512]{2,1,0:T(8,128)(2,1)} %bitcast.159, bf16[1,192,512]{2,1,0:T(8,128)(2,1)} %bitcast.158), kind=kLoop, calls=%fused_computation.181 | loop fusion | flops 196608 | bytes 1179648 | tf_op jit(solution)/shard_map/stack | solution.py:88
  2.0 2.3 %collective-permute-start.2 = (bf16[2,192,512]{2,1,0:T(8,128)(2,1)S(1)}, bf16[2,192,512]{2,1,0:T(8,128)(2,1)S(1)}, u32[]{:S(2)}, u32[]{:S(2)}) collective-permute-start(bf16[2,192,512]{2,1,0:T(8,128)(2,1)S(1)} %get-tuple-element.35), channel_id=1, source_target_pairs={{4,0},{8,4},{12,8},{5,1},{9,5},{13,9},{6,2},{10,6},{14,10},{7,3},{... | collective-permute-start | bytes 1179656 | tf_op jit(solution)/shard_map/ppermute | solution.py:19
  4.3 3.5 %collective-permute-start.1 = (bf16[2,192,512]{2,1,0:T(8,128)(2,1)S(1)}, bf16[2,192,512]{2,1,0:T(8,128)(2,1)S(1)}, u32[]{:S(2)}, u32[]{:S(2)}) collective-permute-start(bf16[2,192,512]{2,1,0:T(8,128)(2,1)S(1)} %get-tuple-element.35), channel_id=1, source_target_pairs={{0,4},{4,8},{8,12},{1,5},{5,9},{9,13},{2,6},{6,10},{10,14},{3,7},{... | collective-permute-start | bytes 1179656 | tf_op jit(solution)/shard_map/ppermute | solution.py:19
  8.0 0.8 reduce-window.8
  9.0 1.7 %convolution_compare_fusion = pred[3,768]{1,0:T(4,128)(4,1)} fusion(s32[768]{0:T(1024)S(1)} %get-tuple-element.44, s32[6,24]{1,0:T(8,128)} %param.11, s32[]{:T(128)S(6)} %select_n.77), kind=kOutput, calls=%fused_computation.34 | convolution fusion | flops 684360 | bytes 7428 | tf_op jit(solution)/shard_map/dot_general | solution.py:33
  10.7 1.6 %convolution_compare_fusion.2 = pred[3,384]{1,0:T(4,128)(4,1)} fusion(s32[384]{0:T(512)S(1)} %get-tuple-element.46, s32[6,24]{1,0:T(8,128)} %param.11, s32[]{:T(128)S(6)} %select_n.77), kind=kOutput, calls=%fused_computation.36 | convolution fusion | flops 342216 | bytes 4740 | tf_op jit(solution)/shard_map/dot_general | solution.py:33
  12.3 0.7 convert_reduce_fusion.4
  13.0 0.7 add_select_fusion.1
  13.7 1.8 %copy.52 = bf16[192,512]{0,1:T(8,128)(2,1)} copy(bf16[192,512]{1,0:T(8,128)(2,1)} %param.8) | data formatting | bytes 393216 | tf_op args[1]
  15.5 1.8 %copy.55 = bf16[192,512]{0,1:T(8,128)(2,1)} copy(bf16[192,512]{1,0:T(8,128)(2,1)} %param.9) | data formatting | bytes 393216 | tf_op args[2]
  17.2 1.1 %copy.54 = bf16[192,512]{0,1:T(8,128)(2,1)S(1)} copy(bf16[192,512]{1,0:T(8,128)(2,1)} %param.7) | data formatting | bytes 393216 | tf_op args[0]
  18.3 1.4 %compare_and_fusion.2 = pred[192,384]{1,0:T(8,128)(4,1)} fusion(s32[384]{0:T(512)S(1)} %convert_reduce_fusion.2, s32[192]{0:T(256)S(1)} %get-tuple-element.7, pred[3,384]{1,0:T(4,128)(4,1)} %convolution_compare_fusion.2), kind=kLoop, calls=%fused_computation.92 | loop fusion | flops 147456 | bytes 77184 | tf_op jit(solution)/shard_map/and | solution.py:34
  19.7 0.7 convert_reduce_fusion
  20.4 1.1 %convolution_compare_fusion.1 = pred[3,768]{1,0:T(4,128)(4,1)S(1)} fusion(s32[768]{0:T(1024)} %get-tuple-element.41, s32[6,24]{1,0:T(8,128)} %param.11, s32[]{:T(128)S(6)} %select_n.77), kind=kOutput, calls=%fused_computation.35 | convolution fusion | flops 684360 | bytes 8452 | tf_op jit(solution)/shard_map/dot_general | solution.py:33
  21.5 1.6 %compare_and_fusion.1 = (pred[192,768]{1,0:T(8,128)(4,1)}, pred[192,768]{1,0:T(8,128)(4,1)}) fusion(s32[768]{0:T(1024)S(1)} %get-tuple-element.9, s32[192]{0:T(256)S(1)} %get-tuple-element.7, s32[768]{0:T(1024)S(1)} %get-tuple-element.8, pred[3,768]{1,0:T(4,128)(4,1)} %convolution_compare_fusion, pred[3,768]{1,0:T(4,128)(4,1)S(1)} %convolution_compare_fusion.1), kind=kLoop, calls=%fused_computation.79 | loop fusion | flops 589824 | bytes 306432 | tf_op jit(solution)/shard_map/and | solution.py:34
  23.2 1.0 pad_maximum_fusion
  24.1 0.4 collective-permute-start.3
  24.6 2.3 %collective-permute-start.5 = (bf16[2,192,512]{2,1,0:T(8,128)(2,1)S(1)}, bf16[2,192,512]{2,1,0:T(8,128)(2,1)}, u32[]{:S(2)}, u32[]{:S(2)}) collective-permute-start(bf16[2,192,512]{2,1,0:T(8,128)(2,1)S(1)} %collective-permute-done.2), channel_id=1, source_target_pairs={{4,0},{8,4},{12,8},{5,1},{9,5},{13,9},{6,2},{10,6},{14,10},{7,3},{... | collective-permute-start | bytes 1179656 | tf_op jit(solution)/shard_map/ppermute | solution.py:19
  26.9 4.2 %collective-permute-start.4 = (bf16[2,192,512]{2,1,0:T(8,128)(2,1)S(1)}, bf16[2,192,512]{2,1,0:T(8,128)(2,1)S(1)}, u32[]{:S(2)}, u32[]{:S(2)}) collective-permute-start(bf16[2,192,512]{2,1,0:T(8,128)(2,1)S(1)} %collective-permute-done.1), channel_id=1, source_target_pairs={{0,4},{4,8},{8,12},{1,5},{5,9},{9,13},{2,6},{6,10},{10,14},{3,7},{... | collective-permute-start | bytes 1179656 | tf_op jit(solution)/shard_map/ppermute | solution.py:19
  31.1 0.8 fusion.129
  31.9 0.8 fusion.128
  32.7 1.8 %fusion.127 = (bf16[1,1,192,512]{3,2,1,0:T(8,128)(2,1)}, bf16[1,1,192,512]{3,2,1,0:T(8,128)(2,1)}) fusion(bf16[1,2,192,512]{3,2,1,0:T(8,128)(2,1)} %collective-permute-done), kind=kLoop, calls=%fused_computation.185 | loop fusion | bytes 786432 | tf_op jit(solution)/shard_map/slice | solution.py:104
  34.5 1.8 %copy.58 = bf16[1,192,512]{1,2,0:T(8,128)(2,1)} copy(bf16[1,192,512]{2,1,0:T(8,128)(2,1)} %get-tuple-element.29) | data formatting | bytes 393216 | tf_op jit(solution)/shard_map/slice | solution.py:103
  36.3 1.8 %copy.57 = bf16[1,192,512]{1,2,0:T(8,128)(2,1)} copy(bf16[1,192,512]{2,1,0:T(8,128)(2,1)} %get-tuple-element.27) | data formatting | bytes 393216 | tf_op jit(solution)/shard_map/slice | solution.py:103
  38.0 1.8 %copy.53 = bf16[1,1,192,512]{2,3,1,0:T(8,128)(2,1)} copy(bf16[1,1,192,512]{3,2,1,0:T(8,128)(2,1)} %get-tuple-element.25) | data formatting | bytes 393216 | tf_op jit(solution)/shard_map/slice | solution.py:103
  39.8 1.8 %copy.62 = bf16[1,192,512]{1,2,0:T(8,128)(2,1)} copy(bf16[1,192,512]{2,1,0:T(8,128)(2,1)} %get-tuple-element.28) | data formatting | bytes 393216 | tf_op jit(solution)/shard_map/slice | solution.py:104
  41.6 1.8 %copy.61 = bf16[1,192,512]{1,2,0:T(8,128)(2,1)} copy(bf16[1,192,512]{2,1,0:T(8,128)(2,1)} %get-tuple-element.26) | data formatting | bytes 393216 | tf_op jit(solution)/shard_map/slice | solution.py:104
  43.3 1.8 %copy.56 = bf16[1,1,192,512]{2,3,1,0:T(8,128)(2,1)} copy(bf16[1,1,192,512]{3,2,1,0:T(8,128)(2,1)} %get-tuple-element.24) | data formatting | bytes 393216 | tf_op jit(solution)/shard_map/slice | solution.py:104
  45.1 3.1 %fusion.12 = (f32[8,192]{1,0:T(8,128)S(1)}, f32[8,384,192]{1,2,0:T(8,128)}) fusion(pred[192,384]{1,0:T(8,128)(4,1)} %compare_and_fusion.2, bf16[192,8,64]{0,2,1:T(8,128)(2,1)S(1)} %bitcast.152, bf16[192,8,64]{0,2,1:T(8,128)(2,1)} %bitcast.156, bf16[192,8,64]{0,2,1:T(8,128)(2,1)} %bitcast.155), kind=kOutput, calls=%fused_computation.16 | convolution fusion | flops 78051840 | bytes 3028992 | tf_op jit(solution)/shard_map/rhd,khd->hrk/dot_general | solution.py:38
  48.2 2.0 %pad_maximum_fusion.1 = bf16[2,2,192,512]{3,2,1,0:T(8,128)(2,1)} fusion(bf16[1,2,192,512]{3,2,1,0:T(8,128)(2,1)} %bitcast.32, bf16[1,2,192,512]{3,2,1,0:T(8,128)(2,1)S(1)} %bitcast.151), kind=kLoop, calls=%fused_computation.61 | loop fusion | flops 393216 | bytes 1572864 | tf_op jit(solution)/shard_map/stack | solution.py:88
  50.2 1.0 %fusion.131 = (bf16[1,192,512]{2,1,0:T(8,128)(2,1)S(1)}, bf16[1,192,512]{2,1,0:T(8,128)(2,1)S(1)}) fusion(bf16[2,192,512]{2,1,0:T(8,128)(2,1)} %collective-permute-done.5), kind=kLoop, calls=%fused_computation.189 | loop fusion | bytes 786432 | tf_op jit(solution)/shard_map/slice | solution.py:104
  51.2 0.8 copy.66
  52.1 0.8 copy.65
  52.9 0.9 copy.70
  53.8 0.8 copy.69
  54.7 1.3 %fusion.125 = (bf16[1,1,192,512]{3,2,1,0:T(8,128)(2,1)S(1)}, bf16[1,1,192,512]{3,2,1,0:T(8,128)(2,1)S(1)}, bf16[1,1,192,512]{3,2,1,0:T(8,128)(2,1)S(1)}, bf16[1,1,192,512]{3,2,1,0:T(8,128)(2,1)S(1)}) fusion(bf16[2,2,192,512]{3,2,1,0:T(8,128)(2,1)} %collective-permute-done.3), kind=kLoop, calls=%fused_computation.183 | loop fusion | bytes 1572864 | tf_op jit(solution)/shard_map/slice | solution.py:104
  55.9 0.8 copy.60
  56.8 0.8 copy.59
  57.6 0.9 copy.64
  58.5 0.8 copy.63
  59.3 4.5 %fusion = (f32[8,192]{1,0:T(8,128)S(1)}, f32[8,768,192]{1,2,0:T(8,128)}) fusion(pred[192,768]{1,0:T(8,128)(4,1)S(1)} %copy-done.3, bf16[192,8,64]{0,2,1:T(8,128)(2,1)S(1)} %bitcast.153, bf16[192,8,64]{0,2,1:T(8,128)(2,1)} %bitcast.176, bf16[192,8,64]{0,2,1:T(8,128)(2,1)} %bitcast.177, bf16[192,8,64]{0,2,1:T(8,128)(2,1)} %bitcast.167, ...), kind=kOutput, calls=%fused_computation.4 | convolution fusion | flops 157678080 | bytes 5855232 | tf_op jit(solution)/shard_map/rhd,khd->hrk/dot_general | solution.py:38
  63.8 1.3 %fusion.126 = (bf16[1,1,192,512]{3,2,1,0:T(8,128)(2,1)S(1)}, bf16[1,1,192,512]{3,2,1,0:T(8,128)(2,1)S(1)}, bf16[1,1,192,512]{3,2,1,0:T(8,128)(2,1)S(1)}, bf16[1,1,192,512]{3,2,1,0:T(8,128)(2,1)S(1)}) fusion(bf16[2,2,192,512]{3,2,1,0:T(8,128)(2,1)} %collective-permute-done.6), kind=kLoop, calls=%fused_computation.184 | loop fusion | bytes 1572864 | tf_op jit(solution)/shard_map/slice | solution.py:104
  65.1 0.8 copy.68
  65.9 0.8 copy.67
  66.8 0.8 copy.72
  67.6 0.8 copy.71
  68.5 2.7 %fusion.1 = (f32[8,192]{1,0:T(8,128)S(1)}, f32[8,768,192]{1,2,0:T(8,128)S(1)}) fusion(pred[192,768]{1,0:T(8,128)(4,1)} %get-tuple-element.50, bf16[192,8,64]{0,2,1:T(8,128)(2,1)S(1)} %bitcast.154, bf16[192,8,64]{0,2,1:T(8,128)(2,1)} %bitcast.174, bf16[192,8,64]{0,2,1:T(8,128)(2,1)} %bitcast.175, bf16[192,8,64]{0,2,1:T(8,128)(2,1)} %bitcast.170, ...), kind=kOutput, calls=%fused_computation.5 | convolution fusion | flops 157678080 | bytes 5855232 | tf_op jit(solution)/shard_map/rhd,khd->hrk/dot_general | solution.py:38
  71.2 1.4 %fusion.4 = f32[8,192]{1,0:T(8,128)S(1)} fusion(f32[8,768,192]{1,2,0:T(8,128)S(1)} %get-tuple-element.52, f32[8,192]{1,0:T(8,128)S(1)} %get-tuple-element.14, pred[192,768]{1,0:T(8,128)(4,1)S(1)} %copy-done.4), kind=kLoop, calls=%fused_computation.8 | loop fusion | flops 5896704 | bytes 4878336 | tf_op jit(solution)/shard_map/reduce_sum | solution.py:48
  72.7 1.4 %fusion.2 = f32[8,192]{1,0:T(8,128)S(1)} fusion(f32[8,768,192]{1,2,0:T(8,128)S(1)} %bitcast.148, f32[8,192]{1,0:T(8,128)S(1)} %get-tuple-element.15, pred[192,768]{1,0:T(8,128)(4,1)S(1)} %copy-done.3), kind=kLoop, calls=%fused_computation.6 | loop fusion | flops 5896704 | bytes 4878336 | tf_op jit(solution)/shard_map/reduce_sum | solution.py:48
  74.2 0.2 copy-done.1
  74.3 0.9 fusion.13
  75.4 1.6 %fusion.18 = f32[192,8,64]{0,2,1:T(8,128)S(1)} fusion(f32[8,768,192]{1,2,0:T(8,128)S(1)} %get-tuple-element.52, f32[8,192]{1,0:T(8,128)S(1)} %get-tuple-element.14, pred[192,768]{1,0:T(8,128)(4,1)S(1)} %copy-done.4, bf16[192,8,64]{0,2,1:T(8,128)(2,1)S(1)} %bitcast.172, bf16[192,8,64]{0,2,1:T(8,128)(2,1)S(1)} %bitcast.173, ...), kind=kOutput, calls=%fused_computation.21 | convolution fusion | flops 160038912 | bytes 6051840 | tf_op jit(solution)/shard_map/hrk,khd->rhd/dot_general | solution.py:49
  77.0 1.8 %fusion.15 = f32[192,8,64]{0,2,1:T(8,128)S(1)} fusion(f32[8,768,192]{1,2,0:T(8,128)S(1)} %bitcast.148, f32[8,192]{1,0:T(8,128)S(1)} %get-tuple-element.15, pred[192,768]{1,0:T(8,128)(4,1)S(1)} %copy-done.3, bf16[192,8,64]{0,2,1:T(8,128)(2,1)S(1)} %bitcast.166, bf16[192,8,64]{0,2,1:T(8,128)(2,1)S(1)} %bitcast.169, bf16[192,8,64]{0,2,1:T(8,128)(2,1)S(1)} %bitcast.162, ...), kind=kOutput, calls=%fused_computation.20 | convolution fusion | flops 160038912 | bytes 6051840 | tf_op jit(solution)/shard_map/hrk,khd->rhd/dot_general | solution.py:49
  78.9 1.0 fusion.27
  79.9 1.9 %collective-permute-start.8 = (bf16[64,512]{0,1:T(8,128)(2,1)S(1)}, bf16[64,512]{0,1:T(8,128)(2,1)S(1)}, u32[]{:S(2)}, u32[]{:S(2)}) collective-permute-start(bf16[64,512]{0,1:T(8,128)(2,1)S(1)} %bitcast.179), channel_id=1, source_target_pairs={{1,0},{4,1},{5,4},{8,5},{9,8},{12,9},{13,12},{3,2},{6,3},{7,6},{10... | collective-permute-start | bytes 196616 | tf_op jit(solution)/shard_map/ppermute | solution.py:19
  81.8 2.4 %collective-permute-start.7 = (bf16[64,512]{0,1:T(8,128)(2,1)S(1)}, bf16[64,512]{0,1:T(8,128)(2,1)S(1)}, u32[]{:S(2)}, u32[]{:S(2)}) collective-permute-start(bf16[64,512]{0,1:T(8,128)(2,1)S(1)} %bitcast.178), channel_id=1, source_target_pairs={{0,1},{1,4},{4,5},{5,8},{8,9},{9,12},{12,13},{2,3},{3,6},{6,7},{7,... | collective-permute-start | bytes 196616 | tf_op jit(solution)/shard_map/ppermute | solution.py:19
  84.3 3.8 %collective-permute-done.7 = bf16[64,512]{0,1:T(8,128)(2,1)S(1)} collective-permute-done((bf16[64,512]{0,1:T(8,128)(2,1)S(1)}, bf16[64,512]{0,1:T(8,128)(2,1)S(1)}, u32[]{:S(2)}, u32[]{:S(2)}) %collective-permute-start.7) | collective-permute-done | bytes 65568 | tf_op jit(solution)/shard_map/ppermute | solution.py:19
  88.1 0.2 pad_maximum_fusion.3
  88.3 1.6 %collective-permute-start.9 = (bf16[320,512]{0,1:T(8,128)(2,1)S(1)}, bf16[320,512]{0,1:T(8,128)(2,1)S(1)}, u32[]{:S(2)}, u32[]{:S(2)}) collective-permute-start(bf16[320,512]{0,1:T(8,128)(2,1)S(1)} %pad_maximum_fusion.3), channel_id=1, source_target_pairs={{0,2},{2,0},{1,3},{3,1},{4,6},{6,4},{5,7},{7,5},{8,10},{10,8},{9,1... | collective-permute-start | bytes 983048 | tf_op jit(solution)/shard_map/ppermute | solution.py:23
  89.9 9.3 %collective-permute-done.9 = bf16[320,512]{0,1:T(8,128)(2,1)S(1)} collective-permute-done((bf16[320,512]{0,1:T(8,128)(2,1)S(1)}, bf16[320,512]{0,1:T(8,128)(2,1)S(1)}, u32[]{:S(2)}, u32[]{:S(2)}) %collective-permute-start.9) | collective-permute-done | bytes 327712 | tf_op jit(solution)/shard_map/ppermute | solution.py:23
  99.2 0.5 fusion.33
  99.7 0.5 convolution_add_fusion
  100.2 0.4 multiply_reduce_fusion
  100.6 0.8 multiply_convert_fusion
  (69 shorter events, 0.7 us)
Async XLA Ops:
  0.0 99.2 %copy-start = (bf16[1024,1024]{1,0:T(8,128)(2,1)S(1)}, bf16[1024,1024]{1,0:T(8,128)(2,1)}, u32[]{:S(2)}) copy-start(bf16[1024,1024]{1,0:T(8,128)(2,1)} %param.12) | copy-start | bytes 6291460
  2.0 21.2 %collective-permute-start.2 = (bf16[2,192,512]{2,1,0:T(8,128)(2,1)S(1)}, bf16[2,192,512]{2,1,0:T(8,128)(2,1)S(1)}, u32[]{:S(2)}, u32[]{:S(2)}) collective-permute-start(bf16[2,192,512]{2,1,0:T(8,128)(2,1)S(1)} %get-tuple-element.35), channel_id=1, source_target_pairs={{4,0},{8,4},{12,8},{5,1},{9,5},{13,9},{6,2},{10,6},{14,10},{7,3},{... | collective-permute-start | bytes 1179656 | tf_op jit(solution)/shard_map/ppermute | solution.py:19
  4.3 18.8 %collective-permute-start.1 = (bf16[2,192,512]{2,1,0:T(8,128)(2,1)S(1)}, bf16[2,192,512]{2,1,0:T(8,128)(2,1)S(1)}, u32[]{:S(2)}, u32[]{:S(2)}) collective-permute-start(bf16[2,192,512]{2,1,0:T(8,128)(2,1)S(1)} %get-tuple-element.35), channel_id=1, source_target_pairs={{0,4},{4,8},{8,12},{1,5},{5,9},{9,13},{2,6},{6,10},{10,14},{3,7},{... | collective-permute-start | bytes 1179656 | tf_op jit(solution)/shard_map/ppermute | solution.py:19
  7.8 24.9 %collective-permute-start = (bf16[1,2,192,512]{3,2,1,0:T(8,128)(2,1)}, bf16[1,2,192,512]{3,2,1,0:T(8,128)(2,1)}, u32[]{:S(2)}, u32[]{:S(2)}) collective-permute-start(bf16[1,2,192,512]{3,2,1,0:T(8,128)(2,1)} %get-tuple-element.34), channel_id=1, source_target_pairs={{0,1},{1,0},{2,3},{3,2},{4,5},{5,4},{6,7},{7,6},{8,9},{9,8},{10,11... | collective-permute-start | bytes 1179656 | tf_op jit(solution)/shard_map/ppermute | solution.py:23
  8.8 6.6 %copy-start.15 = (s32[6,1]{0,1:T(1,128)}, s32[6,1]{0,1:T(1,128)S(1)}, u32[]{:S(2)}) copy-start(s32[6,1]{0,1:T(1,128)S(1)} %reduce-window.8) | copy-start | bytes 76
  24.1 30.5 %collective-permute-start.3 = (bf16[2,2,192,512]{3,2,1,0:T(8,128)(2,1)}, bf16[2,2,192,512]{3,2,1,0:T(8,128)(2,1)}, u32[]{:S(2)}, u32[]{:S(2)}) collective-permute-start(bf16[2,2,192,512]{3,2,1,0:T(8,128)(2,1)} %pad_maximum_fusion), channel_id=1, source_target_pairs={{0,1},{1,0},{2,3},{3,2},{4,5},{5,4},{6,7},{7,6},{8,9},{9,8},{10,11... | collective-permute-start | bytes 2359304 | tf_op jit(solution)/shard_map/ppermute | solution.py:23
  24.6 23.6 %collective-permute-start.5 = (bf16[2,192,512]{2,1,0:T(8,128)(2,1)S(1)}, bf16[2,192,512]{2,1,0:T(8,128)(2,1)}, u32[]{:S(2)}, u32[]{:S(2)}) collective-permute-start(bf16[2,192,512]{2,1,0:T(8,128)(2,1)S(1)} %collective-permute-done.2), channel_id=1, source_target_pairs={{4,0},{8,4},{12,8},{5,1},{9,5},{13,9},{6,2},{10,6},{14,10},{7,3},{... | collective-permute-start | bytes 1179656 | tf_op jit(solution)/shard_map/ppermute | solution.py:19
  26.9 21.3 %collective-permute-start.4 = (bf16[2,192,512]{2,1,0:T(8,128)(2,1)S(1)}, bf16[2,192,512]{2,1,0:T(8,128)(2,1)S(1)}, u32[]{:S(2)}, u32[]{:S(2)}) collective-permute-start(bf16[2,192,512]{2,1,0:T(8,128)(2,1)S(1)} %collective-permute-done.1), channel_id=1, source_target_pairs={{0,4},{4,8},{8,12},{1,5},{5,9},{9,13},{2,6},{6,10},{10,14},{3,7},{... | collective-permute-start | bytes 1179656 | tf_op jit(solution)/shard_map/ppermute | solution.py:19
  50.2 13.7 %collective-permute-start.6 = (bf16[2,2,192,512]{3,2,1,0:T(8,128)(2,1)}, bf16[2,2,192,512]{3,2,1,0:T(8,128)(2,1)}, u32[]{:S(2)}, u32[]{:S(2)}) collective-permute-start(bf16[2,2,192,512]{3,2,1,0:T(8,128)(2,1)} %pad_maximum_fusion.1), channel_id=1, source_target_pairs={{0,1},{1,0},{2,3},{3,2},{4,5},{5,4},{6,7},{7,6},{8,9},{9,8},{10,11... | collective-permute-start | bytes 2359304 | tf_op jit(solution)/shard_map/ppermute | solution.py:23
  52.1 7.2 %copy-start.3 = (pred[192,768]{1,0:T(8,128)(4,1)S(1)}, pred[192,768]{1,0:T(8,128)(4,1)}, u32[]{:S(2)}) copy-start(pred[192,768]{1,0:T(8,128)(4,1)} %get-tuple-element.49) | copy-start | bytes 442372
  67.6 5.0 %slice-start = ((s8[4718592]{0:T(1024)(128)(4,1)}), s8[524288]{0:T(1024)(128)(4,1)S(1)}, s32[]{:S(2)}) async-start(s8[4718592]{0:T(1024)(128)(4,1)} %bitcast.147), calls=%async_computation | async-start | bytes 1048576
  68.5 2.7 %copy-start.4 = (pred[192,768]{1,0:T(8,128)(4,1)S(1)}, pred[192,768]{1,0:T(8,128)(4,1)}, u32[]{:S(2)}) copy-start(pred[192,768]{1,0:T(8,128)(4,1)} %get-tuple-element.50) | copy-start | bytes 442372
  68.5 4.2 %slice-start.1 = ((s8[4718592]{0:T(1024)(128)(4,1)}), s8[4194304]{0:T(1024)(128)(4,1)S(1)}, s32[]{:S(2)}) async-start(s8[4718592]{0:T(1024)(128)(4,1)} %bitcast.147), calls=%async_computation.1 | async-start | bytes 8388608
  72.7 1.7 %copy-start.1 = (f32[8,384,192]{1,2,0:T(8,128)S(1)}, f32[8,384,192]{1,2,0:T(8,128)}, u32[]{:S(2)}) copy-start(f32[8,384,192]{1,2,0:T(8,128)} %get-tuple-element.56) | copy-start | bytes 7077892
  72.7 1.7 %copy-start.2 = (pred[192,384]{1,0:T(8,128)(4,1)S(1)}, pred[192,384]{1,0:T(8,128)(4,1)}, u32[]{:S(2)}) copy-start(pred[192,384]{1,0:T(8,128)(4,1)} %compare_and_fusion.2) | copy-start | bytes 221188
  74.1 1.1 %copy-start.9 = (bf16[1,192,512]{1,2,0:T(8,128)(2,1)S(1)}, bf16[1,192,512]{1,2,0:T(8,128)(2,1)}, u32[]{:S(2)}) copy-start(bf16[1,192,512]{1,2,0:T(8,128)(2,1)} %copy.70) | copy-start | bytes 589828
  74.1 1.1 %copy-start.10 = (bf16[1,192,512]{1,2,0:T(8,128)(2,1)S(1)}, bf16[1,192,512]{1,2,0:T(8,128)(2,1)}, u32[]{:S(2)}) copy-start(bf16[1,192,512]{1,2,0:T(8,128)(2,1)} %copy.69) | copy-start | bytes 589828
  74.1 1.1 %copy-start.13 = (bf16[1,1,192,512]{2,3,1,0:T(8,128)(2,1)S(1)}, bf16[1,1,192,512]{2,3,1,0:T(8,128)(2,1)}, u32[]{:S(2)}) copy-start(bf16[1,1,192,512]{2,3,1,0:T(8,128)(2,1)} %copy.72) | copy-start | bytes 589828
  74.2 1.2 %copy-start.14 = (bf16[1,1,192,512]{2,3,1,0:T(8,128)(2,1)S(1)}, bf16[1,1,192,512]{2,3,1,0:T(8,128)(2,1)}, u32[]{:S(2)}) copy-start(bf16[1,1,192,512]{2,3,1,0:T(8,128)(2,1)} %copy.71) | copy-start | bytes 589828
  75.4 1.6 %copy-start.7 = (bf16[1,192,512]{1,2,0:T(8,128)(2,1)S(1)}, bf16[1,192,512]{1,2,0:T(8,128)(2,1)}, u32[]{:S(2)}) copy-start(bf16[1,192,512]{1,2,0:T(8,128)(2,1)} %copy.62) | copy-start | bytes 589828
  75.4 1.6 %copy-start.8 = (bf16[1,192,512]{1,2,0:T(8,128)(2,1)S(1)}, bf16[1,192,512]{1,2,0:T(8,128)(2,1)}, u32[]{:S(2)}) copy-start(bf16[1,192,512]{1,2,0:T(8,128)(2,1)} %copy.61) | copy-start | bytes 589828
  75.4 1.6 %copy-start.11 = (bf16[1,1,192,512]{2,3,1,0:T(8,128)(2,1)S(1)}, bf16[1,1,192,512]{2,3,1,0:T(8,128)(2,1)}, u32[]{:S(2)}) copy-start(bf16[1,1,192,512]{2,3,1,0:T(8,128)(2,1)} %copy.64) | copy-start | bytes 589828
  75.4 1.6 %copy-start.12 = (bf16[1,1,192,512]{2,3,1,0:T(8,128)(2,1)S(1)}, bf16[1,1,192,512]{2,3,1,0:T(8,128)(2,1)}, u32[]{:S(2)}) copy-start(bf16[1,1,192,512]{2,3,1,0:T(8,128)(2,1)} %copy.63) | copy-start | bytes 589828
  77.0 1.8 %copy-start.5 = (bf16[192,512]{0,1:T(8,128)(2,1)S(1)}, bf16[192,512]{0,1:T(8,128)(2,1)}, u32[]{:S(2)}) copy-start(bf16[192,512]{0,1:T(8,128)(2,1)} %copy.55) | copy-start | bytes 589828
  77.0 1.8 %copy-start.6 = (bf16[1,1,192,512]{2,3,1,0:T(8,128)(2,1)S(1)}, bf16[1,1,192,512]{2,3,1,0:T(8,128)(2,1)}, u32[]{:S(2)}) copy-start(bf16[1,1,192,512]{2,3,1,0:T(8,128)(2,1)} %copy.56) | copy-start | bytes 589828
  78.8 11.0 %copy-start.18 = (bf16[512]{0:T(512)(128)(2,1)S(1)}, bf16[512]{0:T(512)(128)(2,1)}, u32[]{:S(2)}) copy-start(bf16[512]{0:T(512)(128)(2,1)} %param.13) | copy-start | bytes 3076
  78.8 11.0 %copy-start.16 = (s32[192]{0:T(256)S(1)}, s32[192]{0:T(256)}, u32[]{:S(2)}) copy-start(s32[192]{0:T(256)} %get-tuple-element.5) | copy-start | bytes 2308
  78.8 11.0 %copy-start.17 = (s32[192]{0:T(256)S(1)}, s32[192]{0:T(256)}, u32[]{:S(2)}) copy-start(s32[192]{0:T(256)} %get-tuple-element.6) | copy-start | bytes 2308
  79.9 4.4 %collective-permute-start.8 = (bf16[64,512]{0,1:T(8,128)(2,1)S(1)}, bf16[64,512]{0,1:T(8,128)(2,1)S(1)}, u32[]{:S(2)}, u32[]{:S(2)}) collective-permute-start(bf16[64,512]{0,1:T(8,128)(2,1)S(1)} %bitcast.179), channel_id=1, source_target_pairs={{1,0},{4,1},{5,4},{8,5},{9,8},{12,9},{13,12},{3,2},{6,3},{7,6},{10... | collective-permute-start | bytes 196616 | tf_op jit(solution)/shard_map/ppermute | solution.py:19
  81.8 6.3 %collective-permute-start.7 = (bf16[64,512]{0,1:T(8,128)(2,1)S(1)}, bf16[64,512]{0,1:T(8,128)(2,1)S(1)}, u32[]{:S(2)}, u32[]{:S(2)}) collective-permute-start(bf16[64,512]{0,1:T(8,128)(2,1)S(1)} %bitcast.178), channel_id=1, source_target_pairs={{0,1},{1,4},{4,5},{5,8},{8,9},{9,12},{12,13},{2,3},{3,6},{6,7},{7,... | collective-permute-start | bytes 196616 | tf_op jit(solution)/shard_map/ppermute | solution.py:19
  88.3 10.9 %collective-permute-start.9 = (bf16[320,512]{0,1:T(8,128)(2,1)S(1)}, bf16[320,512]{0,1:T(8,128)(2,1)S(1)}, u32[]{:S(2)}, u32[]{:S(2)}) collective-permute-start(bf16[320,512]{0,1:T(8,128)(2,1)S(1)} %pad_maximum_fusion.3), channel_id=1, source_target_pairs={{0,2},{2,0},{1,3},{3,1},{4,6},{6,4},{5,7},{7,5},{8,10},{10,8},{9,1... | collective-permute-start | bytes 983048 | tf_op jit(solution)/shard_map/ppermute | solution.py:23
